TPU v7x, 256 devices: a whole 4x4x8 slice. The times are simulated.
256 devices in a mesh: dp: 4 (over z_hi), expert: 16 (over y, z_lo, core), mp: 4 (over x).
Axes of the slice: x: 4, y: 4, z: 8 (z_hi: 4, z_lo: 2; z = z_hi * 2 + z_lo), core: 2. Of those that a mesh axis runs over, the one named last changes fastest.
Arguments:
- hidden: bfloat16 [16384, 2048], P(('dp', 'expert', 'mp')), may hold values from -6 to 6
- norm_gain: float32 [2048], replicated, may hold values from 0.1 to 1.9
- expert_in: float32 [64, 2048, 2816], P('dp', ('expert', 'mp')), may hold values from -0.125 to 0.125
- expert_out: float32 [64, 2048, 1408], P('dp', ('expert', 'mp')), may hold values from -0.15625 to 0.15625
- expert_ids: int32 [16384, 6], P(('dp', 'expert', 'mp')), may hold values from 0 to 63, all different within a row; in each aligned block of 64 rows (0 to 63, 64 to 127, ...) at most 12 rows name the same one
- gate_levels: int32 [16384, 6], P(('dp', 'expert', 'mp')), may hold values from 1 to 255
- shared_gate: bfloat16 [2048, 2816], P(('dp', 'expert'), 'mp'), may hold values from -0.125 to 0.125
- shared_up: bfloat16 [2048, 2816], P(('dp', 'expert'), 'mp'), may hold values from -0.125 to 0.125
- shared_down: bfloat16 [2048, 2816], P(('dp', 'expert'), 'mp'), may hold values from -0.109375 to 0.109375
- next_gain: float32 [2048], replicated, may hold values from 0.1 to 1.9
- kv_weight: bfloat16 [2048, 576], P(None, 'mp'), may hold values from -0.125 to 0.125
Outputs:
- layer_out: bfloat16 [16384, 2048], P(('dp', 'expert', 'mp'))
- kv_latent: bfloat16 [16384, 576], P(('dp', 'expert'), 'mp')
Inputs may be any that keep to these rules, and one draw needn't show every extreme that they name: `expert_ids`: each row names 6 different experts. Among the 64 rows of one device no expert is named by more than 12 rows, and in every draw some expert is named by exactly 12 rows of some device.
All inputs are finite; a program needn't handle non-finite values.
Results may differ from a plain program's by a relative error of at most 0.012.
Values may be sent and summed in bfloat16 or wider, within the bound.
No kernel may reach another device: no remote copies, remote signals or barrier semaphores. Data moves between devices by JAX's collectives and lax.ppermute only.
A program may use at most 128 MiB of HBM per device.

v0:
```python
import jax
import jax.numpy as jnp
from jax import lax
from jax.sharding import PartitionSpec as P


def rms_scale(values, gain):
    wide = values.astype(jnp.float32)
    mean_sq = jnp.mean(wide * wide, axis=-1, keepdims=True)
    return (wide * lax.rsqrt(mean_sq + 1e-06) * gain).astype(jnp.bfloat16)


def expert_part(rows, gate_up_w, down_w):
    quarter = down_w.shape[1]
    gate_up = jnp.dot(rows, gate_up_w, preferred_element_type=jnp.float32)
    act = (jax.nn.silu(gate_up[:, :quarter]) * gate_up[:, quarter:]).astype(jnp.bfloat16)
    return lax.dot_general(
        act, down_w, (((1,), (1,)), ((), ())), preferred_element_type=jnp.float32
    )


def on_device(
    hidden,
    norm_gain,
    expert_in,
    expert_out,
    expert_ids,
    gate_levels,
    shared_gate,
    shared_up,
    shared_down,
    next_gain,
    kv_weight,
):
    tok_rows, width = hidden.shape
    top = expert_ids.shape[1]
    n_mp = lax.axis_size("mp")
    n_groups = lax.axis_size(("dp", "expert"))
    capacity = min(tok_rows, (2 * tok_rows * top + n_groups - 1) // n_groups)
    local_e, local_rows, double = expert_in.shape
    full_ff = double // 2
    quarter = full_ff // n_mp
    in_cast = (
        expert_in.astype(jnp.bfloat16)
        .reshape(local_e, local_rows, 2, n_mp, quarter)
        .transpose(0, 3, 1, 2, 4)
    )
    out_cast = (
        expert_out.astype(jnp.bfloat16)
        .reshape(local_e, local_rows, n_mp, quarter)
        .transpose(0, 2, 1, 3)
    )
    in_send = in_cast.reshape(local_e * n_mp, local_rows, 2, quarter)
    out_send = out_cast.reshape(local_e * n_mp, local_rows, quarter)
    in_recv, out_recv = (
        lax.all_to_all(in_send, ("expert", "mp"), split_axis=0, concat_axis=1, tiled=True),
        lax.all_to_all(out_send, ("expert", "mp"), split_axis=0, concat_axis=1, tiled=True),
    )
    gate_up_w = in_recv.reshape(width, 2 * quarter)
    down_w = out_recv.reshape(width, quarter)
    normed = rms_scale(hidden, norm_gain)
    levels = gate_levels.astype(jnp.float32)
    gate_weights = levels / jnp.sum(levels, axis=1, keepdims=True)
    flat_ids = expert_ids.reshape(-1)
    pairs = flat_ids.shape[0]
    onehot = (flat_ids[:, None] == jnp.arange(n_groups, dtype=jnp.int32)[None, :]).astype(jnp.int32)
    before = jnp.cumsum(onehot, axis=0) - onehot
    slot_of_pair = jnp.sum(before * onehot, axis=1)
    target = flat_ids * capacity + slot_of_pair
    token_of_pair = jnp.arange(pairs, dtype=jnp.int32) // top
    slot_ids = jnp.arange(n_groups * capacity, dtype=jnp.int32)
    token_slot = target.reshape(tok_rows, top)[:, :, None] == slot_ids[None, None, :]
    slot_token = jnp.any(token_slot, axis=1).astype(jnp.bfloat16)
    send = lax.dot_general(
        slot_token, normed, (((0,), (0,)), ((), ())), preferred_element_type=jnp.float32
    ).astype(jnp.bfloat16)
    bounds = (0, 2 * capacity // 3, capacity) if capacity >= 3 else (0, capacity)
    spans = list(zip(bounds[:-1], bounds[1:]))
    send = send.reshape(n_groups, capacity, width)
    received = [
        lax.all_to_all(send[:, lo:hi], ("dp", "expert"), split_axis=0, concat_axis=0, tiled=True)
        for lo, hi in spans
    ]
    shared_cols = shared_gate.shape[1]
    shared_cat = jnp.concatenate([shared_gate, shared_up, shared_down], axis=1)
    shared_cat = lax.all_gather(shared_cat, "dp", axis=0, tiled=False)
    shared_cat = lax.all_gather(shared_cat, "expert", axis=1, tiled=False)
    shared_cat = shared_cat.reshape(width, 3 * shared_cols)
    group_rows = lax.all_gather(normed, "mp", axis=0, tiled=True)
    kv_cols = kv_weight.shape[1]
    kv_full = lax.all_to_all(
        jnp.broadcast_to(kv_weight[None], (n_mp,) + kv_weight.shape), "mp", 0, 0, tiled=True
    )
    received[0], shared_cat, group_rows, kv_full = lax.optimization_barrier(
        (received[0], shared_cat, group_rows, kv_full)
    )
    back = []
    for c, (lo, hi) in enumerate(spans):
        chunk = hi - lo
        slots_here = received[c].reshape(n_groups * chunk, width)
        rows = lax.all_gather(slots_here, "mp", axis=0, tiled=True)
        summed = lax.psum_scatter(
            expert_part(rows, gate_up_w, down_w).astype(jnp.bfloat16),
            "mp",
            scatter_dimension=0,
            tiled=True,
        )
        back.append(
            lax.all_to_all(
                summed.reshape(n_groups, chunk, width),
                ("dp", "expert"),
                split_axis=0,
                concat_axis=0,
                tiled=True,
            )
        )
    back = jnp.concatenate(back, axis=1).reshape(n_groups * capacity, width)
    slot_weight = jnp.sum(jnp.where(token_slot, gate_weights[:, :, None], 0.0), axis=1)
    routed = jnp.dot(
        slot_weight,
        back.astype(jnp.float32),
        precision=lax.Precision.HIGHEST,
        preferred_element_type=jnp.float32,
    )
    gate_w = shared_cat[:, :shared_cols]
    up_w = shared_cat[:, shared_cols : 2 * shared_cols]
    down_s = shared_cat[:, 2 * shared_cols :]
    rows = group_rows
    gate_part = jnp.dot(rows, gate_w, preferred_element_type=jnp.float32)
    up_part = jnp.dot(rows, up_w, preferred_element_type=jnp.float32)
    act = (jax.nn.silu(gate_part) * up_part).astype(jnp.bfloat16)
    shared_out = lax.psum_scatter(
        lax.dot_general(act, down_s, (((1,), (1,)), ((), ())), preferred_element_type=jnp.float32),
        "mp",
        scatter_dimension=0,
        tiled=True,
    )
    layer_out = (hidden.astype(jnp.float32) + routed + shared_out).astype(jnp.bfloat16)
    next_rows = rms_scale(layer_out, next_gain)
    kv_full = kv_full.transpose(1, 0, 2).reshape(width, n_mp * kv_cols)
    kv_local = jnp.dot(next_rows, kv_full, preferred_element_type=jnp.float32).astype(jnp.bfloat16)
    kv_send = kv_local.reshape(tok_rows, n_mp, kv_cols).transpose(1, 0, 2)
    kv_latent = lax.all_to_all(kv_send, "mp", 0, 0, tiled=True).reshape(n_mp * tok_rows, kv_cols)
    return (layer_out, kv_latent)


def solution(mesh):
    in_specs = (
        P(("dp", "expert", "mp"), None),
        P(),
        P("dp", ("expert", "mp"), None),
        P("dp", ("expert", "mp"), None),
        P(("dp", "expert", "mp"), None),
        P(("dp", "expert", "mp"), None),
        P(("dp", "expert"), "mp"),
        P(("dp", "expert"), "mp"),
        P(("dp", "expert"), "mp"),
        P(),
        P(None, "mp"),
    )
    out_specs = (P(("dp", "expert", "mp"), None), P(("dp", "expert"), "mp"))
    return jax.shard_map(
        on_device, mesh=mesh, in_specs=in_specs, out_specs=out_specs, check_vma=False
    )
```

profile of v0, /device:TPU:8, one launch (start us, length us, event | category | flops | bytes accessed | tf_op | source)
XLA Modules:
  0.0 541.9 jit_solution(3544073971727459353)
XLA Ops:
  7.2 1.1 fusion.31
  8.3 1.8 fusion.33
  10.2 1.0 concatenate.9
  11.2 21.2 %all-gather = bf16[128,2112]{1,0:T(8,128)(2,1)} all-gather(bf16[32,2112]{1,0:T(8,128)(2,1)S(1)} %concatenate.9), channel_id=2, replica_groups=mesh['dp'=4,'expert'=16,'mp'=4] {'dp'}, dimensions={0}, use_global_device_ids=true | all-gather | bytes 675840 | tf_op jit(solution)/shard_map/all_gather | solution.py:86
  32.5 0.8 copy.54
  33.5 0.9 reduce-window.6
  35.3 2.0 convolution_convert_fusion.2
  37.3 2.8 reshape.104
  40.1 2.1 slice.68
  42.2 42.6 %all_to_all.48 = bf16[64,4,2048]{2,1,0:T(4,128)(2,1)S(1)} all-to-all(bf16[64,4,2048]{2,1,0:T(4,128)(2,1)S(1)} %slice.68), channel_id=1, replica_groups=mesh['dp'=4,'expert'=16,'mp'=4] {'dp','expert'}, dimensions={0} | all-to-all | bytes 2097152 | tf_op jit(solution)/shard_map/all_to_all | solution.py:81
  84.8 1.1 reshape.113
  85.9 1.7 broadcast_in_dim.12
  87.6 4.3 all-to-all-start.1
  91.9 3.2 slice.61
  95.1 26.2 %all-to-all-done.1 = bf16[4,2048,144]{1,2,0:T(8,128)(2,1)S(1)} async-done(((bf16[4,2048,144]{1,2,0:T(8,128)(2,1)}), bf16[4,2048,144]{1,2,0:T(8,128)(2,1)S(1)}, u32[]{:S(2)}, u32[]{:S(2)}) %all-to-all-start.1) | async-done | bytes 2359328 | tf_op jit(solution)/shard_map/all_to_all | solution.py:91
  121.3 9.8 %all-to-all-start = ((bf16[64,8,2048]{2,1,0:T(8,128)(2,1)}), bf16[64,8,2048]{2,1,0:T(8,128)(2,1)}, u32[]{:S(2)}, u32[]{:S(2)}) async-start(bf16[64,8,2048]{2,1,0:T(8,128)(2,1)} %slice.61), calls=%async_computation | async-start | bytes 4194304 | tf_op jit(solution)/shard_map/all_to_all | solution.py:81
  131.2 51.1 %all-to-all-done = bf16[64,8,2048]{2,1,0:T(8,128)(2,1)} async-done(((bf16[64,8,2048]{2,1,0:T(8,128)(2,1)}), bf16[64,8,2048]{2,1,0:T(8,128)(2,1)}, u32[]{:S(2)}, u32[]{:S(2)}) %all-to-all-start) | async-done | bytes 2097184 | tf_op jit(solution)/shard_map/all_to_all | solution.py:81
  182.3 4.6 convert_element_type.61
  186.9 6.8 %reshape.107 = bf16[16,32,2,4,352]{4,3,2,1,0:T(4,128)(2,1)S(1)} reshape(bf16[16,32,2816]{2,1,0:T(8,128)(2,1)} %convert_element_type.61) | data formatting | bytes 5767168 | tf_op jit(solution)/shard_map/reshape | solution.py:45
  193.7 2.4 copy.58
  196.1 6.0 %all-to-all-start.2 = ((bf16[64,32,2,352]{3,1,2,0:T(8,128)(2,1)}), bf16[64,32,2,352]{3,1,2,0:T(8,128)(2,1)S(1)}, u32[]{:S(2)}, u32[]{:S(2)}) async-start(bf16[64,32,2,352]{3,1,2,0:T(8,128)(2,1)} %bitcast.48), calls=%async_computation.2 | async-start | bytes 6291456 | tf_op jit(solution)/shard_map/all_to_all | solution.py:56
  202.0 2.0 convert_element_type.63
  204.5 1.4 pad_maximum_fusion.1
  205.9 48.5 %all-to-all-done.2 = bf16[64,32,2,352]{3,1,2,0:T(8,128)(2,1)S(1)} async-done(((bf16[64,32,2,352]{3,1,2,0:T(8,128)(2,1)}), bf16[64,32,2,352]{3,1,2,0:T(8,128)(2,1)S(1)}, u32[]{:S(2)}, u32[]{:S(2)}) %all-to-all-start.2) | async-done | bytes 2883616 | tf_op jit(solution)/shard_map/all_to_all | solution.py:56
  254.4 9.1 %all-to-all-start.3 = ((bf16[64,32,352]{2,1,0:T(8,128)(2,1)}), bf16[64,32,352]{2,1,0:T(8,128)(2,1)}, u32[]{:S(2)}, u32[]{:S(2)}) async-start(bf16[64,32,352]{2,1,0:T(8,128)(2,1)} %bitcast.51), calls=%async_computation.3 | async-start | bytes 3145728 | tf_op jit(solution)/shard_map/all_to_all | solution.py:57
  264.0 4.9 copy.59
  268.9 6.4 %reshape.109 = bf16[2048,704]{1,0:T(8,128)(2,1)S(1)} reshape(bf16[64,32,2,352]{3,2,1,0:T(2,128)(2,1)} %copy.59) | data formatting | bytes 5767168 | tf_op jit(solution)/shard_map/reshape | solution.py:59
  275.4 7.0 %fusion.47 = f32[1024,704]{0,1:T(8,128)} fusion(bf16[1024,2048]{1,0:T(8,128)(2,1)} %all-gather.11.cloned.1.call-done, bf16[2048,704]{1,0:T(8,128)(2,1)S(1)} %reshape.109), kind=kOutput, calls=%fused_computation.64 | convolution fusion | flops 2952790016 | bytes 9961472 | tf_op jit(solution)/shard_map/dot_general | solution.py:15
  282.4 10.2 %all-to-all-done.3 = bf16[64,32,352]{2,1,0:T(8,128)(2,1)} async-done(((bf16[64,32,352]{2,1,0:T(8,128)(2,1)}), bf16[64,32,352]{2,1,0:T(8,128)(2,1)}, u32[]{:S(2)}, u32[]{:S(2)}) %all-to-all-start.3) | async-done | bytes 1441824 | tf_op jit(solution)/shard_map/all_to_all | solution.py:57
  292.6 6.7 %convolution_convert_fusion.1 = bf16[1024,2048]{1,0:T(8,128)(2,1)} fusion(bf16[2048,352]{1,0:T(8,128)(2,1)} %bitcast.7, f32[1024,704]{0,1:T(8,128)} %fusion.47), kind=kOutput, calls=%fused_computation.2 | convolution fusion | flops 1480654848 | bytes 8519680 | tf_op jit(solution)/shard_map/dot_general | solution.py:17
  299.6 13.5 %all-gather.9.cloned.1.call-done = bf16[2048,2048]{1,0:T(8,128)(2,1)} async-done(((bf16[512,2048]{1,0:T(8,128)(2,1)}), bf16[2048,2048]{1,0:T(8,128)(2,1)}) %all-gather.9.cloned.1.call-update) | async-done | bytes 8388624 | tf_op jit(solution)/shard_map/all_gather | solution.py:101
  313.0 8.8 %fusion.46 = f32[2048,704]{0,1:T(8,128)S(1)} fusion(bf16[2048,2048]{1,0:T(8,128)(2,1)} %all-gather.9.cloned.1.call-done, bf16[2048,704]{1,0:T(8,128)(2,1)S(1)} %reshape.109), kind=kOutput, calls=%fused_computation.63 | convolution fusion | flops 5905580032 | bytes 17039360 | tf_op jit(solution)/shard_map/dot_general | solution.py:15
  321.9 8.3 %convolution_convert_fusion = bf16[2048,2048]{1,0:T(8,128)(2,1)} fusion(bf16[2048,352]{1,0:T(8,128)(2,1)} %bitcast.7, f32[2048,704]{0,1:T(8,128)S(1)} %fusion.46), kind=kOutput, calls=%fused_computation | convolution fusion | flops 2961309696 | bytes 15597568 | tf_op jit(solution)/shard_map/dot_general | solution.py:17
  330.2 35.6 %reduce-scatter.6.cloned.1.call-done = bf16[256,2048]{1,0:T(8,128)(2,1)} async-done(((bf16[1024,2048]{1,0:T(8,128)(2,1)}), bf16[256,2048]{1,0:T(8,128)(2,1)}) %reduce-scatter.6.cloned.1.call-update) | async-done | bytes 1048592 | tf_op jit(solution)/shard_map/reduce_scatter | solution.py:102
  365.8 2.2 reshape.114
  368.0 10.6 %all-to-all-start.6 = ((bf16[64,4,2048]{2,1,0:T(4,128)(2,1)}), bf16[64,4,2048]{2,1,0:T(4,128)(2,1)S(1)}, u32[]{:S(2)}, u32[]{:S(2)}) async-start(bf16[64,4,2048]{2,1,0:T(4,128)(2,1)} %reshape.114), calls=%async_computation.8 | async-start | bytes 2097152 | tf_op jit(solution)/shard_map/all_to_all | solution.py:109
  378.6 4.8 fusion.4
  383.4 24.0 %all-to-all-done.6 = bf16[64,4,2048]{2,1,0:T(4,128)(2,1)S(1)} async-done(((bf16[64,4,2048]{2,1,0:T(4,128)(2,1)}), bf16[64,4,2048]{2,1,0:T(4,128)(2,1)S(1)}, u32[]{:S(2)}, u32[]{:S(2)}) %all-to-all-start.6) | async-done | bytes 1048608 | tf_op jit(solution)/shard_map/all_to_all | solution.py:109
  407.4 43.8 %reduce-scatter.4.cloned.1.call-done = bf16[512,2048]{1,0:T(8,128)(2,1)} async-done(((bf16[2048,2048]{1,0:T(8,128)(2,1)}), bf16[512,2048]{1,0:T(8,128)(2,1)}) %reduce-scatter.4.cloned.1.call-update) | async-done | bytes 2097168 | tf_op jit(solution)/shard_map/reduce_scatter | solution.py:102
  451.2 10.6 %all-to-all-start.4 = ((bf16[64,8,2048]{2,1,0:T(8,128)(2,1)}), bf16[64,8,2048]{2,1,0:T(8,128)(2,1)S(1)}, u32[]{:S(2)}, u32[]{:S(2)}) async-start(bf16[64,8,2048]{2,1,0:T(8,128)(2,1)} %bitcast.53), calls=%async_computation.5 | async-start | bytes 4194304 | tf_op jit(solution)/shard_map/all_to_all | solution.py:109
  462.1 9.2 %fusion = f32[256,2048]{1,0:T(8,128)} fusion(bf16[2048,2112]{1,0:T(8,128)(2,1)} %bitcast.58, bf16[256,2048]{1,0:T(8,128)(2,1)} %all-gather.7.cloned.1.call-done, f32[256,704]{0,1:T(8,128)} %fusion.4), kind=kOutput, calls=%fused_computation.4 | convolution fusion | flops 1477476352 | bytes 10158080 | tf_op jit(solution)/shard_map/dot_general | solution.py:133
  471.4 0.9 select_reduce_fusion
  472.3 40.8 %all-to-all-done.4 = bf16[64,8,2048]{2,1,0:T(8,128)(2,1)S(1)} async-done(((bf16[64,8,2048]{2,1,0:T(8,128)(2,1)}), bf16[64,8,2048]{2,1,0:T(8,128)(2,1)S(1)}, u32[]{:S(2)}, u32[]{:S(2)}) %all-to-all-start.4) | async-done | bytes 2097184 | tf_op jit(solution)/shard_map/all_to_all | solution.py:109
  513.1 2.7 pad_maximum_fusion
  515.8 4.8 reshape.115
  520.6 3.2 fusion.28
  524.5 0.8 convolution_convert_fusion.3
  525.5 8.5 %all_to_all.49 = bf16[4,64,144]{2,1,0:T(8,128)(2,1)S(1)} all-to-all(bf16[4,64,144]{2,1,0:T(8,128)(2,1)S(1)} %bitcast.54), channel_id=1, replica_groups=mesh['dp'=4,'expert'=16,'mp'=4] {'mp'}, dimensions={0} | all-to-all | bytes 147456 | tf_op jit(solution)/shard_map/all_to_all | solution.py:143
  (54 shorter events, 4.6 us)
Async XLA Ops:
  7.2 27.9 %copy-start.5 = (s32[64,6]{0,1:T(8,128)S(1)}, s32[64,6]{0,1:T(8,128)}, u32[]{:S(2)}) copy-start(s32[64,6]{0,1:T(8,128)} %param.15) | copy-start | bytes 4612
  7.2 124.0 %all-gather.7.cloned.1.call-start = ((), (), s32[]{:S(2)}) async-start(), calls=%async_computation.11 | async-start | bytes 1310720 | tf_op jit(solution)/shard_map/all_gather | solution.py:89
  10.2 172.1 %all-gather.13.cloned.1.call-start = ((), (), s32[]{:S(2)}) async-start(), calls=%async_computation.17 | async-start | bytes 9469952 | tf_op jit(solution)/shard_map/all_gather | solution.py:87
  32.4 243.0 %all-gather.11.cloned.1.call-start = ((), (), s32[]{:S(2)}) async-start(), calls=%async_computation.14 | async-start | bytes 5242880 | tf_op jit(solution)/shard_map/all_gather | solution.py:101
  42.2 43.7 %copy-start.4 = (bf16[2048,144]{0,1:T(8,128)(2,1)S(1)}, bf16[2048,144]{0,1:T(8,128)(2,1)}, u32[]{:S(2)}) copy-start(bf16[2048,144]{0,1:T(8,128)(2,1)} %param.21) | copy-start | bytes 1769476
  87.6 33.7 %all-to-all-start.1 = ((bf16[4,2048,144]{1,2,0:T(8,128)(2,1)}), bf16[4,2048,144]{1,2,0:T(8,128)(2,1)S(1)}, u32[]{:S(2)}, u32[]{:S(2)}) async-start(bf16[4,2048,144]{1,2,0:T(8,128)(2,1)} %broadcast_in_dim.12), calls=%async_computation.1 | async-start | bytes 4718592 | tf_op jit(solution)/shard_map/all_to_all | solution.py:91
  121.3 61.0 %copy-start = (bf16[4,2048,144]{1,2,0:T(8,128)(2,1)}, bf16[4,2048,144]{1,2,0:T(8,128)(2,1)S(1)}, u32[]{:S(2)}) copy-start(bf16[4,2048,144]{1,2,0:T(8,128)(2,1)S(1)} %all-to-all-done.1) | copy-start | bytes 7077892
  121.3 61.0 %all-to-all-start = ((bf16[64,8,2048]{2,1,0:T(8,128)(2,1)}), bf16[64,8,2048]{2,1,0:T(8,128)(2,1)}, u32[]{:S(2)}, u32[]{:S(2)}) async-start(bf16[64,8,2048]{2,1,0:T(8,128)(2,1)} %slice.61), calls=%async_computation | async-start | bytes 4194304 | tf_op jit(solution)/shard_map/all_to_all | solution.py:81
  131.1 181.9 %all-gather.9.cloned.1.call-start = ((), (), s32[]{:S(2)}) async-start(), calls=%async_computation.12 | async-start | bytes 10485760 | tf_op jit(solution)/shard_map/all_gather | solution.py:101
  196.1 58.3 %all-to-all-start.2 = ((bf16[64,32,2,352]{3,1,2,0:T(8,128)(2,1)}), bf16[64,32,2,352]{3,1,2,0:T(8,128)(2,1)S(1)}, u32[]{:S(2)}, u32[]{:S(2)}) async-start(bf16[64,32,2,352]{3,1,2,0:T(8,128)(2,1)} %bitcast.48), calls=%async_computation.2 | async-start | bytes 6291456 | tf_op jit(solution)/shard_map/all_to_all | solution.py:56
  254.4 38.2 %all-to-all-start.3 = ((bf16[64,32,352]{2,1,0:T(8,128)(2,1)}), bf16[64,32,352]{2,1,0:T(8,128)(2,1)}, u32[]{:S(2)}, u32[]{:S(2)}) async-start(bf16[64,32,352]{2,1,0:T(8,128)(2,1)} %bitcast.51), calls=%async_computation.3 | async-start | bytes 3145728 | tf_op jit(solution)/shard_map/all_to_all | solution.py:57
  263.5 102.3 %reduce-scatter.6.cloned.1.call-start = ((), (), s32[]{:S(2)}) async-start(), calls=%async_computation.15 | async-start | bytes 5242880 | tf_op jit(solution)/shard_map/reduce_scatter | solution.py:102
  299.3 151.9 %reduce-scatter.4.cloned.1.call-start = ((), (), s32[]{:S(2)}) async-start(), calls=%async_computation.13 | async-start | bytes 10485760 | tf_op jit(solution)/shard_map/reduce_scatter | solution.py:102
  330.2 48.4 %copy-start.8 = (bf16[256,2048]{1,0:T(8,128)(2,1)S(1)}, bf16[256,2048]{1,0:T(8,128)(2,1)}, u32[]{:S(2)}) copy-start(bf16[256,2048]{1,0:T(8,128)(2,1)} %all-gather.7.cloned.1.call-done) | copy-start | bytes 3145732
  368.0 39.4 %all-to-all-start.6 = ((bf16[64,4,2048]{2,1,0:T(4,128)(2,1)}), bf16[64,4,2048]{2,1,0:T(4,128)(2,1)S(1)}, u32[]{:S(2)}, u32[]{:S(2)}) async-start(bf16[64,4,2048]{2,1,0:T(4,128)(2,1)} %reshape.114), calls=%async_computation.8 | async-start | bytes 2097152 | tf_op jit(solution)/shard_map/all_to_all | solution.py:109
  451.2 61.8 %all-to-all-start.4 = ((bf16[64,8,2048]{2,1,0:T(8,128)(2,1)}), bf16[64,8,2048]{2,1,0:T(8,128)(2,1)S(1)}, u32[]{:S(2)}, u32[]{:S(2)}) async-start(bf16[64,8,2048]{2,1,0:T(8,128)(2,1)} %bitcast.53), calls=%async_computation.5 | async-start | bytes 4194304 | tf_op jit(solution)/shard_map/all_to_all | solution.py:109
  461.8 9.5 %copy-start.6 = (s32[64,6]{0,1:T(8,128)S(1)}, s32[64,6]{0,1:T(8,128)}, u32[]{:S(2)}) copy-start(s32[64,6]{0,1:T(8,128)} %param.16) | copy-start | bytes 4612
  461.8 58.8 %reduce-scatter.8.cloned.1.call-start = ((), (), s32[]{:S(2)}) async-start(), calls=%async_computation.16 | async-start | bytes 2621440 | tf_op jit(solution)/shard_map/reduce_scatter | solution.py:132
  515.8 4.8 copy-start.2
  520.6 3.9 copy-start.7
  520.6 3.9 copy-start.1
  523.8 0.7 copy-start.3
Sparse Core Ops, SparseCore 0:
  10.4 29.3 all-gather.6
  41.6 74.7 all-gather.12
  118.2 53.2 all-gather.10
  182.4 130.5 all-gather.8
  315.4 50.3 reduce-scatter.5
  368.4 82.7 reduce-scatter.3
  471.5 31.7 reduce-scatter.7
where the time goes:
time: 551 us; the launch traced here: 542 us
  waiting for transfers between devices  294 us (53%)
  blocking collectives  72.3 us (13%)
  starting transfers between devices  51.4 us (9%)
  matrix products  50.9 us (9%)
  local copies, waits for them, and re-layouts  42.9 us (8%)
  other arithmetic  15.9 us (3%)
  between operations  14.7 us (3%)
    reduce_scatter x2, waiting for transfers between devices, on_device(): lax.psum_scatter(expert_part(rows, gate_up_w, down_w).astype(jnp.bfloat16...  79.4 us
    all_to_all x2, waiting for transfers between devices, on_device(): lax.all_to_all(summed.reshape(n_groups, chunk, width), ('dp', 'expert'),...  64.8 us
    all_to_all x1, waiting for transfers between devices, on_device(): lax.all_to_all(send[:, lo:hi], ('dp', 'expert'), split_axis=0, concat_axi...  51.1 us
    all_to_all x1, waiting for transfers between devices, on_device(): lax.all_to_all(in_send, ('expert', 'mp'), split_axis=0, concat_axis=1, ti...  48.5 us
    all_to_all x1, blocking collectives, on_device(): lax.all_to_all(send[:, lo:hi], ('dp', 'expert'), split_axis=0, concat_axi...  42.6 us
    all_to_all x1, waiting for transfers between devices, on_device(): lax.all_to_all(jnp.broadcast_to(kv_weight[None], (n_mp,) + kv_weight.shap...  26.2 us
    all_gather x1, blocking collectives, on_device(): shared_cat = lax.all_gather(shared_cat, 'dp', axis=0, tiled=False)  21.2 us
    all_to_all x2, starting transfers between devices, on_device(): lax.all_to_all(summed.reshape(n_groups, chunk, width), ('dp', 'expert'),...  21.1 us
  transfers between devices with their start and end apart: 13, of which 9 were waited for; matrix products, arithmetic and copies ran while one was open for 19% of the time, Pallas kernels for 0%

commit v1 on v0

--- a/solution.py
+++ b/solution.py
@@ -98,7 +98,9 @@
     for c, (lo, hi) in enumerate(spans):
         chunk = hi - lo
         slots_here = received[c].reshape(n_groups * chunk, width)
-        rows = lax.all_gather(slots_here, "mp", axis=0, tiled=True)
+        row_out = jnp.stack([slots_here for _ in range(lax.axis_size("mp"))], axis=0)
+        main = lax.all_to_all(row_out, "mp", 0, 0)
+        rows = jnp.concatenate(main, axis=0)
         summed = lax.psum_scatter(
             expert_part(rows, gate_up_w, down_w).astype(jnp.bfloat16),
             "mp",

time: 551 us -> 653 us (1.19)
  waiting for transfers between devices: 294 us -> 398 us
  blocking collectives: 72.3 us -> 46.3 us
  starting transfers between devices: 51.4 us -> 69.9 us
  local copies, waits for them, and re-layouts: 42.9 us -> 54.1 us
    all_to_all x0 -> x2, waiting for transfers between devices: none -> 156 us  [on_device(): main = lax.all_to_all(row_out, 'mp', 0, 0)]
    all_to_all x1 -> x0, blocking collectives: 42.6 us -> none  [on_device(): lax.all_to_all(send[:, lo:hi], ('dp', 'expert'), split_axis=0, concat_axi...]
    reduce_scatter x2, waiting for transfers between devices: 79.4 us -> 40.9 us  [on_device(): lax.psum_scatter(expert_part(rows, gate_up_w, down_w).astype(jnp.bfloat16...]
    all_gather x1, blocking collectives: 21.2 us -> 37.8 us  [on_device(): shared_cat = lax.all_gather(shared_cat, 'dp', axis=0, tiled=False)]
    all_to_all x1, waiting for transfers between devices: 10.2 us -> 25.9 us  [on_device(): lax.all_to_all(out_send, ('expert', 'mp'), split_axis=0, concat_axis=1, t...]
    all_gather x2 -> x0, waiting for transfers between devices: 13.5 us -> none  [on_device(): rows = lax.all_gather(slots_here, 'mp', axis=0, tiled=True)]
    all_to_all x1, waiting for transfers between devices: 48.5 us -> 36.3 us  [on_device(): lax.all_to_all(in_send, ('expert', 'mp'), split_axis=0, concat_axis=1, ti...]
    another operation x1 -> x4, local copies, waits for them, and re-layouts: 0.48 us -> 12.3 us  [the longest x3 11.9 us: on_device(): jnp.stack([slots_here for _ in range(lax.axis_size('mp'))], axis=0)]
  transfers between devices with their start and end apart: 13 -> 14, of which waited for: 9 -> 9; matrix products, arithmetic and copies ran while one was open for 19% -> 15% of each run, Pallas kernels for 0% -> 0%
where the time goes in v1:
time: 653 us; the launch traced here: 644 us
  waiting for transfers between devices  398 us (61%)
  starting transfers between devices  69.9 us (11%)
  local copies, waits for them, and re-layouts  54.1 us (8%)
  matrix products  46.3 us (7%)
  blocking collectives  46.3 us (7%)
  between operations  14.4 us (2%)
  other arithmetic  14 us (2%)
    all_to_all x2, waiting for transfers between devices, on_device(): main = lax.all_to_all(row_out, 'mp', 0, 0)  156 us
    all_to_all x2, waiting for transfers between devices, on_device(): lax.all_to_all(summed.reshape(n_groups, chunk, width), ('dp', 'expert'),...  65.6 us
    all_to_all x2, waiting for transfers between devices, on_device(): lax.all_to_all(send[:, lo:hi], ('dp', 'expert'), split_axis=0, concat_axi...  54.8 us
    reduce_scatter x2, waiting for transfers between devices, on_device(): lax.psum_scatter(expert_part(rows, gate_up_w, down_w).astype(jnp.bfloat16...  40.9 us
    all_gather x1, blocking collectives, on_device(): shared_cat = lax.all_gather(shared_cat, 'dp', axis=0, tiled=False)  37.8 us
    all_to_all x1, waiting for transfers between devices, on_device(): lax.all_to_all(in_send, ('expert', 'mp'), split_axis=0, concat_axis=1, ti...  36.3 us
    all_to_all x1, waiting for transfers between devices, on_device(): lax.all_to_all(out_send, ('expert', 'mp'), split_axis=0, concat_axis=1, t...  25.9 us
    all_to_all x2, starting transfers between devices, on_device(): lax.all_to_all(send[:, lo:hi], ('dp', 'expert'), split_axis=0, concat_axi...  21 us
  transfers between devices with their start and end apart: 14, of which 9 were waited for; matrix products, arithmetic and copies ran while one was open for 15% of the time, Pallas kernels for 0%

profile of v1, /device:TPU:8, one launch (start us, length us, event | category | flops | bytes accessed | tf_op | source)
XLA Modules:
  0.0 643.6 jit_solution(10284468769924234417)
XLA Ops:
  7.2 2.8 broadcast_in_dim.12
  10.0 4.6 all-to-all-start.1
  15.0 0.9 reduce-window.6
  17.8 2.0 convolution_convert_fusion.2
  19.8 2.7 reshape.108
  22.5 3.2 slice.68
  25.7 18.4 %all-to-all-done.1 = bf16[4,2048,144]{1,2,0:T(8,128)(2,1)} async-done(((bf16[4,2048,144]{1,2,0:T(8,128)(2,1)}), bf16[4,2048,144]{1,2,0:T(8,128)(2,1)}, u32[]{:S(2)}, u32[]{:S(2)}) %all-to-all-start.1) | async-done | bytes 2359328 | tf_op jit(solution)/shard_map/all_to_all | solution.py:91
  44.1 12.1 %all-to-all-start.6 = ((bf16[64,4,2048]{2,1,0:T(4,128)(2,1)}), bf16[64,4,2048]{2,1,0:T(4,128)(2,1)S(1)}, u32[]{:S(2)}, u32[]{:S(2)}) async-start(bf16[64,4,2048]{2,1,0:T(4,128)(2,1)} %slice.68), calls=%async_computation.7 | async-start | bytes 2097152 | tf_op jit(solution)/shard_map/all_to_all | solution.py:81
  57.1 37.8 %all-gather = bf16[128,2112]{1,0:T(8,128)(2,1)} all-gather(bf16[32,2112]{1,0:T(8,128)(2,1)S(1)} %concatenate.9), channel_id=2, replica_groups=mesh['dp'=4,'expert'=16,'mp'=4] {'dp'}, dimensions={0}, use_global_device_ids=true | all-gather | bytes 675840 | tf_op jit(solution)/shard_map/all_gather | solution.py:86
  95.0 2.0 convert_element_type.63
  97.4 1.4 pad_maximum_fusion.1
  98.8 5.8 all-to-all-start.4
  104.6 3.1 slice.61
  107.8 25.9 %all-to-all-done.4 = bf16[64,32,352]{2,1,0:T(8,128)(2,1)S(1)} async-done(((bf16[64,32,352]{2,1,0:T(8,128)(2,1)}), bf16[64,32,352]{2,1,0:T(8,128)(2,1)S(1)}, u32[]{:S(2)}, u32[]{:S(2)}) %all-to-all-start.4) | async-done | bytes 1441824 | tf_op jit(solution)/shard_map/all_to_all | solution.py:57
  133.7 8.9 %all-to-all-start = ((bf16[64,8,2048]{2,1,0:T(8,128)(2,1)}), bf16[64,8,2048]{2,1,0:T(8,128)(2,1)}, u32[]{:S(2)}, u32[]{:S(2)}) async-start(bf16[64,8,2048]{2,1,0:T(8,128)(2,1)} %slice.61), calls=%async_computation | async-start | bytes 4194304 | tf_op jit(solution)/shard_map/all_to_all | solution.py:81
  142.7 4.7 convert_element_type.61
  147.3 6.6 %reshape.111 = bf16[16,32,2,4,352]{4,3,2,1,0:T(4,128)(2,1)S(1)} reshape(bf16[16,32,2816]{2,1,0:T(8,128)(2,1)} %convert_element_type.61) | data formatting | bytes 5767168 | tf_op jit(solution)/shard_map/reshape | solution.py:45
  154.0 2.4 copy.58
  156.3 54.8 %all-to-all-done = bf16[64,8,2048]{2,1,0:T(8,128)(2,1)} async-done(((bf16[64,8,2048]{2,1,0:T(8,128)(2,1)}), bf16[64,8,2048]{2,1,0:T(8,128)(2,1)}, u32[]{:S(2)}, u32[]{:S(2)}) %all-to-all-start) | async-done | bytes 2097184 | tf_op jit(solution)/shard_map/all_to_all | solution.py:81
  211.1 9.2 %all-to-all-start.3 = ((bf16[64,32,2,352]{3,1,2,0:T(8,128)(2,1)}), bf16[64,32,2,352]{3,1,2,0:T(8,128)(2,1)S(1)}, u32[]{:S(2)}, u32[]{:S(2)}) async-start(bf16[64,32,2,352]{3,1,2,0:T(8,128)(2,1)} %bitcast.50), calls=%async_computation.3 | async-start | bytes 6291456 | tf_op jit(solution)/shard_map/all_to_all | solution.py:56
  220.3 2.1 stack_reshape.5
  222.5 36.3 %all-to-all-done.3 = bf16[64,32,2,352]{3,1,2,0:T(8,128)(2,1)S(1)} async-done(((bf16[64,32,2,352]{3,1,2,0:T(8,128)(2,1)}), bf16[64,32,2,352]{3,1,2,0:T(8,128)(2,1)S(1)}, u32[]{:S(2)}, u32[]{:S(2)}) %all-to-all-start.3) | async-done | bytes 2883616 | tf_op jit(solution)/shard_map/all_to_all | solution.py:56
  258.8 3.8 stack.7
  262.6 5.3 all-to-all-start.7
  267.9 4.9 copy.59
  272.8 6.4 %reshape.113 = bf16[2048,704]{1,0:T(8,128)(2,1)S(1)} reshape(bf16[64,32,2,352]{3,2,1,0:T(2,128)(2,1)} %copy.59) | data formatting | bytes 5767168 | tf_op jit(solution)/shard_map/reshape | solution.py:59
  279.3 38.2 %all-to-all-done.7 = bf16[4,256,2048]{2,1,0:T(8,128)(2,1)} async-done(((bf16[4,256,2048]{2,1,0:T(8,128)(2,1)}), bf16[4,256,2048]{2,1,0:T(8,128)(2,1)}, u32[]{:S(2)}, u32[]{:S(2)}) %all-to-all-start.7) | async-done | bytes 4194336 | tf_op jit(solution)/shard_map/all_to_all | solution.py:102
  317.5 5.9 stack.6
  323.5 5.7 all-to-all-start.2
  329.2 5.1 fusion.47
  334.3 4.5 convolution_convert_fusion.1
  339.1 117.5 %all-to-all-done.2 = bf16[4,512,2048]{2,1,0:T(8,128)(2,1)} async-done(((bf16[4,512,2048]{2,1,0:T(8,128)(2,1)}), bf16[4,512,2048]{2,1,0:T(8,128)(2,1)}, u32[]{:S(2)}, u32[]{:S(2)}) %all-to-all-start.2) | async-done | bytes 8388640 | tf_op jit(solution)/shard_map/all_to_all | solution.py:102
  456.6 8.9 %fusion.46 = f32[2048,704]{0,1:T(8,128)S(1)} fusion(bf16[2048,2048]{1,0:T(8,128)(2,1)} %bitcast.4, bf16[2048,704]{1,0:T(8,128)(2,1)S(1)} %reshape.113), kind=kOutput, calls=%fused_computation.63 | convolution fusion | flops 5905580032 | bytes 17039360 | tf_op jit(solution)/shard_map/dot_general | solution.py:15
  465.6 7.0 %convolution_convert_fusion = bf16[2048,2048]{1,0:T(8,128)(2,1)} fusion(bf16[2048,352]{1,0:T(8,128)(2,1)S(1)} %bitcast.55, f32[2048,704]{0,1:T(8,128)S(1)} %fusion.46), kind=kOutput, calls=%fused_computation | convolution fusion | flops 2961309696 | bytes 15597568 | tf_op jit(solution)/shard_map/dot_general | solution.py:17
  472.7 2.4 reshape.118
  475.0 7.1 %all-to-all-start.8 = ((bf16[64,4,2048]{2,1,0:T(4,128)(2,1)}), bf16[64,4,2048]{2,1,0:T(4,128)(2,1)S(1)}, u32[]{:S(2)}, u32[]{:S(2)}) async-start(bf16[64,4,2048]{2,1,0:T(4,128)(2,1)} %reshape.118), calls=%async_computation.10 | async-start | bytes 2097152 | tf_op jit(solution)/shard_map/all_to_all | solution.py:111
  482.1 4.1 fusion.4
  486.2 24.7 %all-to-all-done.8 = bf16[64,4,2048]{2,1,0:T(4,128)(2,1)S(1)} async-done(((bf16[64,4,2048]{2,1,0:T(4,128)(2,1)}), bf16[64,4,2048]{2,1,0:T(4,128)(2,1)S(1)}, u32[]{:S(2)}, u32[]{:S(2)}) %all-to-all-start.8) | async-done | bytes 1048608 | tf_op jit(solution)/shard_map/all_to_all | solution.py:111
  510.9 40.9 %reduce-scatter.4.cloned.1.call-done = bf16[512,2048]{1,0:T(8,128)(2,1)} async-done(((bf16[2048,2048]{1,0:T(8,128)(2,1)}), bf16[512,2048]{1,0:T(8,128)(2,1)}) %reduce-scatter.4.cloned.1.call-update) | async-done | bytes 2097168 | tf_op jit(solution)/shard_map/reduce_scatter | solution.py:104
  551.8 10.6 %all-to-all-start.5 = ((bf16[64,8,2048]{2,1,0:T(8,128)(2,1)}), bf16[64,8,2048]{2,1,0:T(8,128)(2,1)S(1)}, u32[]{:S(2)}, u32[]{:S(2)}) async-start(bf16[64,8,2048]{2,1,0:T(8,128)(2,1)} %bitcast.53), calls=%async_computation.6 | async-start | bytes 4194304 | tf_op jit(solution)/shard_map/all_to_all | solution.py:111
  562.7 9.2 %fusion = f32[256,2048]{1,0:T(8,128)} fusion(bf16[2048,2112]{1,0:T(8,128)(2,1)} %bitcast.60, bf16[256,2048]{1,0:T(8,128)(2,1)} %all-gather.5.cloned.1.call-done, f32[256,704]{0,1:T(8,128)} %fusion.4), kind=kOutput, calls=%fused_computation.4 | convolution fusion | flops 1477476352 | bytes 10158080 | tf_op jit(solution)/shard_map/dot_general | solution.py:135
  571.9 0.9 select_reduce_fusion
  572.8 40.9 %all-to-all-done.5 = bf16[64,8,2048]{2,1,0:T(8,128)(2,1)S(1)} async-done(((bf16[64,8,2048]{2,1,0:T(8,128)(2,1)}), bf16[64,8,2048]{2,1,0:T(8,128)(2,1)S(1)}, u32[]{:S(2)}, u32[]{:S(2)}) %all-to-all-start.5) | async-done | bytes 2097184 | tf_op jit(solution)/shard_map/all_to_all | solution.py:111
  613.7 2.7 pad_maximum_fusion
  616.4 4.7 reshape.119
  621.2 3.0 fusion.28
  624.9 2.5 convolution_convert_fusion.3
  627.6 8.5 %all_to_all.58 = bf16[4,64,144]{2,1,0:T(8,128)(2,1)S(1)} all-to-all(bf16[4,64,144]{2,1,0:T(8,128)(2,1)S(1)} %bitcast.56), channel_id=1, replica_groups=mesh['dp'=4,'expert'=16,'mp'=4] {'mp'}, dimensions={0} | all-to-all | bytes 147456 | tf_op jit(solution)/shard_map/all_to_all | solution.py:145
  (65 shorter events, 5.9 us)
Async XLA Ops:
  7.2 7.4 %copy-start.9 = (s32[64,6]{0,1:T(8,128)S(1)}, s32[64,6]{0,1:T(8,128)}, u32[]{:S(2)}) copy-start(s32[64,6]{0,1:T(8,128)} %param.15) | copy-start | bytes 4612
  10.0 6.8 %copy-start.1 = (bf16[64,2048]{1,0:T(8,128)(2,1)S(1)}, bf16[64,2048]{1,0:T(8,128)(2,1)}, u32[]{:S(2)}) copy-start(bf16[64,2048]{1,0:T(8,128)(2,1)} %param.11) | copy-start | bytes 786436
  10.0 7.0 %copy-start.11 = (f32[2048]{0:T(1024)S(1)}, f32[2048]{0:T(1024)}, u32[]{:S(2)}) copy-start(f32[2048]{0:T(1024)} %param.12) | copy-start | bytes 24580
  10.0 34.1 %all-to-all-start.1 = ((bf16[4,2048,144]{1,2,0:T(8,128)(2,1)}), bf16[4,2048,144]{1,2,0:T(8,128)(2,1)}, u32[]{:S(2)}, u32[]{:S(2)}) async-start(bf16[4,2048,144]{1,2,0:T(8,128)(2,1)} %broadcast_in_dim.12), calls=%async_computation.1 | async-start | bytes 4718592 | tf_op jit(solution)/shard_map/all_to_all | solution.py:91
  22.5 34.5 %copy-start.6 = (bf16[32,704]{1,0:T(8,128)(2,1)S(1)}, bf16[32,704]{1,0:T(8,128)(2,1)}, u32[]{:S(2)}) copy-start(bf16[32,704]{1,0:T(8,128)(2,1)} %param.17) | copy-start | bytes 135172
  22.5 34.5 %copy-start.7 = (bf16[32,704]{1,0:T(8,128)(2,1)S(1)}, bf16[32,704]{1,0:T(8,128)(2,1)}, u32[]{:S(2)}) copy-start(bf16[32,704]{1,0:T(8,128)(2,1)} %param.18) | copy-start | bytes 135172
  22.5 34.5 %copy-start.8 = (bf16[32,704]{1,0:T(8,128)(2,1)S(1)}, bf16[32,704]{1,0:T(8,128)(2,1)}, u32[]{:S(2)}) copy-start(bf16[32,704]{1,0:T(8,128)(2,1)} %param.19) | copy-start | bytes 135172
  44.1 54.7 %all-to-all-start.6 = ((bf16[64,4,2048]{2,1,0:T(4,128)(2,1)}), bf16[64,4,2048]{2,1,0:T(4,128)(2,1)S(1)}, u32[]{:S(2)}, u32[]{:S(2)}) async-start(bf16[64,4,2048]{2,1,0:T(4,128)(2,1)} %slice.68), calls=%async_computation.7 | async-start | bytes 2097152 | tf_op jit(solution)/shard_map/all_to_all | solution.py:81
  56.2 223.1 %all-gather.5.cloned.1.call-start = ((), (), s32[]{:S(2)}) async-start(), calls=%async_computation.13 | async-start | bytes 1310720 | tf_op jit(solution)/shard_map/all_gather | solution.py:89
  56.9 222.4 %all-gather.7.cloned.1.call-start = ((), (), s32[]{:S(2)}) async-start(), calls=%async_computation.17 | async-start | bytes 9469952 | tf_op jit(solution)/shard_map/all_gather | solution.py:87
  98.8 9.0 %copy-start = (bf16[64,4,2048]{2,1,0:T(4,128)(2,1)}, bf16[64,4,2048]{2,1,0:T(4,128)(2,1)S(1)}, u32[]{:S(2)}) copy-start(bf16[64,4,2048]{2,1,0:T(4,128)(2,1)S(1)} %all-to-all-done.6) | copy-start | bytes 3145732
  98.8 34.9 %all-to-all-start.4 = ((bf16[64,32,352]{2,1,0:T(8,128)(2,1)}), bf16[64,32,352]{2,1,0:T(8,128)(2,1)S(1)}, u32[]{:S(2)}, u32[]{:S(2)}) async-start(bf16[64,32,352]{2,1,0:T(8,128)(2,1)} %bitcast.7), calls=%async_computation.4 | async-start | bytes 3145728 | tf_op jit(solution)/shard_map/all_to_all | solution.py:57
  133.7 8.9 %copy-start.2 = (bf16[64,32,352]{2,1,0:T(8,128)(2,1)}, bf16[64,32,352]{2,1,0:T(8,128)(2,1)S(1)}, u32[]{:S(2)}) copy-start(bf16[64,32,352]{2,1,0:T(8,128)(2,1)S(1)} %all-to-all-done.4) | copy-start | bytes 4325380
  133.7 77.4 %all-to-all-start = ((bf16[64,8,2048]{2,1,0:T(8,128)(2,1)}), bf16[64,8,2048]{2,1,0:T(8,128)(2,1)}, u32[]{:S(2)}, u32[]{:S(2)}) async-start(bf16[64,8,2048]{2,1,0:T(8,128)(2,1)} %slice.61), calls=%async_computation | async-start | bytes 4194304 | tf_op jit(solution)/shard_map/all_to_all | solution.py:81
  211.1 47.7 %all-to-all-start.3 = ((bf16[64,32,2,352]{3,1,2,0:T(8,128)(2,1)}), bf16[64,32,2,352]{3,1,2,0:T(8,128)(2,1)S(1)}, u32[]{:S(2)}, u32[]{:S(2)}) async-start(bf16[64,32,2,352]{3,1,2,0:T(8,128)(2,1)} %bitcast.50), calls=%async_computation.3 | async-start | bytes 6291456 | tf_op jit(solution)/shard_map/all_to_all | solution.py:56
  262.6 55.0 %all-to-all-start.7 = ((bf16[4,256,2048]{2,1,0:T(8,128)(2,1)}), bf16[4,256,2048]{2,1,0:T(8,128)(2,1)}, u32[]{:S(2)}, u32[]{:S(2)}) async-start(bf16[4,256,2048]{2,1,0:T(8,128)(2,1)} %stack.7), calls=%async_computation.8 | async-start | bytes 8388608 | tf_op jit(solution)/shard_map/all_to_all | solution.py:102
  323.5 133.2 %all-to-all-start.2 = ((bf16[4,512,2048]{2,1,0:T(8,128)(2,1)}), bf16[4,512,2048]{2,1,0:T(8,128)(2,1)}, u32[]{:S(2)}, u32[]{:S(2)}) async-start(bf16[4,512,2048]{2,1,0:T(8,128)(2,1)} %stack.6), calls=%async_computation.2 | async-start | bytes 16777216 | tf_op jit(solution)/shard_map/all_to_all | solution.py:102
  329.1 143.5 %reduce-scatter.6.cloned.1.call-start = ((), (), s32[]{:S(2)}) async-start(), calls=%async_computation.15 | async-start | bytes 5242880 | tf_op jit(solution)/shard_map/reduce_scatter | solution.py:104
  329.2 5.2 copy-start.3
  338.9 213.0 %reduce-scatter.4.cloned.1.call-start = ((), (), s32[]{:S(2)}) async-start(), calls=%async_computation.14 | async-start | bytes 10485760 | tf_op jit(solution)/shard_map/reduce_scatter | solution.py:104
  456.6 9.0 %copy-start.4 = (bf16[64,32,352]{2,1,0:T(8,128)(2,1)S(1)}, bf16[64,32,352]{2,1,0:T(8,128)(2,1)}, u32[]{:S(2)}) copy-start(bf16[64,32,352]{2,1,0:T(8,128)(2,1)} %copy-done.2) | copy-start | bytes 4325380
  472.6 9.5 %copy-start.13 = (bf16[256,2048]{1,0:T(8,128)(2,1)S(1)}, bf16[256,2048]{1,0:T(8,128)(2,1)}, u32[]{:S(2)}) copy-start(bf16[256,2048]{1,0:T(8,128)(2,1)} %all-gather.5.cloned.1.call-done) | copy-start | bytes 3145732
  475.0 35.9 %all-to-all-start.8 = ((bf16[64,4,2048]{2,1,0:T(4,128)(2,1)}), bf16[64,4,2048]{2,1,0:T(4,128)(2,1)S(1)}, u32[]{:S(2)}, u32[]{:S(2)}) async-start(bf16[64,4,2048]{2,1,0:T(4,128)(2,1)} %reshape.118), calls=%async_computation.10 | async-start | bytes 2097152 | tf_op jit(solution)/shard_map/all_to_all | solution.py:111
  551.8 61.8 %all-to-all-start.5 = ((bf16[64,8,2048]{2,1,0:T(8,128)(2,1)}), bf16[64,8,2048]{2,1,0:T(8,128)(2,1)S(1)}, u32[]{:S(2)}, u32[]{:S(2)}) async-start(bf16[64,8,2048]{2,1,0:T(8,128)(2,1)} %bitcast.53), calls=%async_computation.6 | async-start | bytes 4194304 | tf_op jit(solution)/shard_map/all_to_all | solution.py:111
  562.4 9.5 %copy-start.10 = (s32[64,6]{0,1:T(8,128)S(1)}, s32[64,6]{0,1:T(8,128)}, u32[]{:S(2)}) copy-start(s32[64,6]{0,1:T(8,128)} %param.16) | copy-start | bytes 4612
  562.4 58.8 %reduce-scatter.8.cloned.1.call-start = ((), (), s32[]{:S(2)}) async-start(), calls=%async_computation.16 | async-start | bytes 2621440 | tf_op jit(solution)/shard_map/reduce_scatter | solution.py:134
  621.1 3.8 copy-start.12
  624.2 0.7 copy-start.5
Sparse Core Ops, SparseCore 0:
  59.4 25.7 all-gather.4
  95.1 99.3 all-gather.6
  339.0 80.5 reduce-scatter.5
  472.7 79.0 reduce-scatter.3
  572.0 31.7 reduce-scatter.7
